TPU v7x, 32 devices: a whole 2x2x4 slice. The times are simulated.
32 devices in a mesh: outer: 8 (over z, y), inner: 4 (over x, core).
Axes of the slice: x: 2, y: 2, z: 4, core: 2. Of those that a mesh axis runs over, the one named last changes fastest.
Arguments:
- qkv_blocks: bfloat16 [4096, 16, 512], P(('outer', 'inner')), may hold values from -4 to 4
- block_scales: bfloat16 [128, 16, 4], P(('outer', 'inner')), may hold values from 0.25 to 4
- gate_logits: bfloat16 [4096, 16, 4], P(('outer', 'inner')), may hold values from -5 to 45056
- conv_weight: float32 [4, 16, 512], P(None, 'inner'), may hold values from -3 to 3
- decay_log: float32 [32], P('inner'), may hold values from -15 to -3
- dt_bias: float32 [32], P('inner'), may hold values from -1 to 1
- norm_gain: float32 [128], replicated, may hold values from 0.5 to 1.5
Outputs:
- normed_heads: bfloat16 [4096, 32, 128], P(('outer', 'inner'))
All inputs are finite; a program needn't handle non-finite values.
Results may differ from a plain program's by a relative error of at most 0.0004.
Values may be sent and summed in bfloat16 or wider, within the bound.
No kernel may reach another device: no remote copies, remote signals or barrier semaphores. Data moves between devices by JAX's collectives and lax.ppermute only.
A program may use at most 128 MiB of HBM per device.

v0:
```python
import jax
import jax.numpy as jnp
from jax import lax
from jax.sharding import PartitionSpec as P

HD = 128
BLOCK = 128
QB = 32
CONV = 4
HIGH_PRECISION = lax.Precision.HIGHEST
EPS_NORM = 1e-06


def from_behind(value, axis, steps):
    count = lax.axis_size(axis)
    leading, last = (max(0, -steps), min(count, count - steps))
    return lax.ppermute(value, axis, [(source, source + steps) for source in range(leading, last)])


def carried_in(part, axis, combine, identity):
    place = lax.axis_index(axis)
    gathered = jax.tree.map(lambda a: lax.all_gather(a, axis), part)
    state = jax.tree.map(lambda a, e: jnp.zeros_like(a) + jnp.asarray(e, a.dtype), part, identity)

    def one(lap, state):
        return combine(
            state, jax.tree.map(lambda a: lax.dynamic_index_in_dim(a, lap, 0, False), gathered)
        )

    return lax.fori_loop(0, place, one, state)


def dequantize(blocks, scales):
    token_count = blocks.shape[0]
    head_count = blocks.shape[1]
    quarter = blocks.shape[2] // 4
    shaped = blocks.astype(jnp.float32).reshape(token_count // QB, QB, head_count, 4, quarter)
    scaled = shaped * scales.astype(jnp.float32)[:, None, :, :, None]
    return scaled.reshape(token_count, head_count, 4 * quarter)


def convolve(extended, conv_weight, token_count):
    summed = conv_weight[0] * extended[0:token_count]
    for offset in range(1, CONV):
        summed = summed + conv_weight[offset] * extended[offset : offset + token_count]
    return jax.nn.silu(summed)


def unit_rows(matrix):
    return matrix * lax.rsqrt(jnp.sum(matrix * matrix, axis=-1, keepdims=True) + EPS_NORM)


def split_heads(mixed, gate_share, decay_log, dt_bias):
    token_count = mixed.shape[0]
    value_heads = 2 * mixed.shape[1]
    block_count = token_count // BLOCK
    queries = jnp.repeat(unit_rows(mixed[:, :, :HD]), 2, axis=1)
    keys_in = jnp.repeat(unit_rows(mixed[:, :, HD : 2 * HD]), 2, axis=1)
    values_in = mixed[:, :, 2 * HD :].reshape(token_count, value_heads, HD)
    gate_values = gate_share.astype(jnp.float32)
    beta_gate = jax.nn.sigmoid(gate_values[:, :, :2].reshape(token_count, value_heads))
    raw_decay = gate_values[:, :, 2:].reshape(token_count, value_heads)
    log_decay = -jnp.exp(decay_log) * jax.nn.softplus(raw_decay + dt_bias)

    def blocked(tensor):
        return jnp.swapaxes(tensor.reshape((block_count, BLOCK) + tensor.shape[1:]), 1, 2)

    return (
        blocked(queries),
        blocked(keys_in),
        blocked(values_in),
        blocked(beta_gate),
        blocked(log_decay),
    )


def lower_inverse(strict_part, length):
    negated = -strict_part
    eye_block = jnp.eye(length, dtype=jnp.float32)
    inverse = eye_block + negated
    power = negated
    for unused_level in range((length - 1).bit_length() - 1):
        power = jnp.einsum("...ij,...jk->...ik", power, power, precision=HIGH_PRECISION)
        inverse = inverse + jnp.einsum(
            "...ij,...jk->...ik", inverse, power, precision=HIGH_PRECISION
        )
    return inverse


def block_terms(queries, keys_in, values_in, beta_gate, log_decay):
    cumulative = jnp.cumsum(log_decay, axis=-1)
    length = log_decay.shape[-1]
    row_index = lax.broadcasted_iota(jnp.int32, (length, length), 0)
    col_index = lax.broadcasted_iota(jnp.int32, (length, length), 1)
    lower_mask = row_index >= col_index
    strict = row_index > col_index
    differ = cumulative[..., :, None] - cumulative[..., None, :]
    weights = jnp.where(lower_mask, jnp.exp(jnp.where(lower_mask, differ, 0.0)), 0.0)
    key_dots = jnp.einsum("...cd,...ed->...ce", keys_in, keys_in, precision=HIGH_PRECISION)
    strict_part = jnp.where(strict, key_dots * weights * beta_gate[..., :, None], 0.0)
    growth = jnp.exp(cumulative)
    right_side = jnp.concatenate(
        [beta_gate[..., None] * values_in, (beta_gate * growth)[..., None] * keys_in], axis=-1
    )
    inverse = lower_inverse(strict_part, length)
    solved = jnp.einsum("...ce,...ed->...cd", inverse, right_side, precision=HIGH_PRECISION)
    head_width = values_in.shape[-1]
    update_part = solved[..., :head_width]
    write_part = solved[..., head_width:]
    attend = jnp.einsum("...cd,...ed->...ce", queries, keys_in, precision=HIGH_PRECISION) * weights
    final_sum = cumulative[..., -1]
    carried_keys = jnp.exp(final_sum[..., None] - cumulative)[..., None] * keys_in
    return (
        update_part,
        write_part,
        attend,
        growth[..., None] * queries,
        carried_keys,
        jnp.exp(final_sum),
    )


def block_output(update_part, write_part, attend, grown_query, current_state):
    incoming_value_rows = update_part - jnp.einsum(
        "...ck,...kv->...cv", write_part, current_state, precision=HIGH_PRECISION
    )
    result = jnp.einsum("...ck,...kv->...cv", grown_query, current_state, precision=HIGH_PRECISION)
    result = result + jnp.einsum(
        "...ce,...ev->...cv", attend, incoming_value_rows, precision=HIGH_PRECISION
    )
    return (result, incoming_value_rows)


def advance(current_state, incoming_value_rows, carried_keys, decay_total):
    return decay_total[..., None, None] * current_state + jnp.einsum(
        "...ck,...cv->...kv", carried_keys, incoming_value_rows, precision=HIGH_PRECISION
    )


def compose(earlier, later):
    trans_early, state_early = earlier
    trans_late, state_late = later
    joined_trans = jnp.einsum("hij,hjk->hik", trans_late, trans_early, precision=HIGH_PRECISION)
    joined_state = (
        jnp.einsum("hij,hjk->hik", trans_late, state_early, precision=HIGH_PRECISION) + state_late
    )
    return (joined_trans, joined_state)


def pair_update(passed_block_state, inputs):
    current_update, current_write, carried_now, decay_now = inputs
    target_values = jnp.concatenate([current_update, jnp.zeros_like(current_update)], axis=-1)
    incoming_value_rows = target_values - jnp.einsum(
        "zsg,zgj->zsj", current_write, passed_block_state, precision=HIGH_PRECISION
    )
    return advance(passed_block_state, incoming_value_rows, carried_now, decay_now)


def step_drop(passed_block_state, inputs):
    return (pair_update(passed_block_state, inputs), None)


def step_state(current_state, inputs):
    current_update, current_write, carried_now, decay_now = inputs
    incoming_value_rows = current_update - jnp.einsum(
        "zsg,zgj->zsj", current_write, current_state, precision=HIGH_PRECISION
    )
    return (advance(current_state, incoming_value_rows, carried_now, decay_now), current_state)


def local(qkv_blocks, block_scales, gate_logits, conv_weight, decay_log, dt_bias, norm_gain):
    coded_share, scale_share, gate_share = (
        lax.all_to_all(qkv_blocks, "inner", split_axis=1, concat_axis=0, tiled=True),
        lax.all_to_all(block_scales, "inner", split_axis=1, concat_axis=0, tiled=True),
        lax.all_to_all(gate_logits, "inner", split_axis=1, concat_axis=0, tiled=True),
    )
    regrouped = dequantize(coded_share, scale_share)
    token_count = regrouped.shape[0]
    previous = from_behind(regrouped[token_count - CONV + 1 :], "outer", 1)
    mixed = convolve(jnp.concatenate([previous, regrouped], axis=0), conv_weight, token_count)
    queries, keys_in, values_in, beta_gate, log_decay = split_heads(
        mixed, gate_share, decay_log, dt_bias
    )
    update_part, write_part, attend, grown_query, carried_keys, decay_total = block_terms(
        queries, keys_in, values_in, beta_gate, log_decay
    )
    head_count = queries.shape[1]
    zero_state = jnp.zeros((head_count, HD, HD), jnp.float32)
    identity = jnp.broadcast_to(jnp.eye(HD, dtype=jnp.float32), (head_count, HD, HD))
    start_pair = jnp.concatenate([zero_state, identity], axis=-1)
    sequence = (update_part, write_part, carried_keys, decay_total)
    final_pair, unused_steps = lax.scan(step_drop, start_pair, sequence)
    prefix = carried_in(
        (final_pair[..., HD:], final_pair[..., :HD]), "outer", compose, (identity, zero_state)
    )
    incoming = prefix[1]
    unused_final, starts = lax.scan(step_state, incoming, sequence)
    outputs, unused_values = block_output(update_part, write_part, attend, grown_query, starts)
    scaled = (
        outputs
        * lax.rsqrt(jnp.mean(outputs * outputs, axis=-1, keepdims=True) + EPS_NORM)
        * norm_gain
    )
    normed = scaled.astype(jnp.bfloat16)
    by_token = jnp.swapaxes(normed, 1, 2).reshape(token_count, head_count, HD)
    return lax.all_to_all(by_token, "inner", split_axis=0, concat_axis=1, tiled=True)


def solution(mesh):
    placed = (
        P(("outer", "inner"), None, None),
        P(("outer", "inner"), None, None),
        P(("outer", "inner"), None, None),
        P(None, "inner", None),
        P("inner"),
        P("inner"),
        P(),
    )
    return jax.shard_map(
        local,
        mesh=mesh,
        in_specs=placed,
        out_specs=P(("outer", "inner"), None, None),
        check_vma=False,
    )
```

profile of v0, /device:TPU:28, one launch (start us, length us, event | category | flops | bytes accessed | tf_op | source)
XLA Modules:
  0.0 353.2 jit_solution(18354611735783497234)
XLA Ops:
  7.3 6.4 %all_to_all.45 = bf16[4,16,4]{2,0,1:T(4,128)(2,1)S(1)} all-to-all(bf16[4,16,4]{2,0,1:T(4,128)(2,1)S(1)} %copy.45), channel_id=1, replica_groups=mesh['outer'=8,'inner'=4] {'inner'}, dimensions={1} | all-to-all | bytes 1024 | tf_op jit(solution)/shard_map/all_to_all | solution.py:174
  13.8 3.3 all-to-all-start
  17.0 4.1 %copy.43 = bf16[128,16,512]{2,0,1:T(8,128)(2,1)} copy(bf16[128,16,512]{2,1,0:T(8,128)(2,1)} %param.13) | data formatting | bytes 4194304 | tf_op args[0]
  21.2 3.6 %all-to-all-start.1 = ((bf16[128,16,512]{2,0,1:T(8,128)(2,1)}), bf16[128,16,512]{2,0,1:T(8,128)(2,1)S(1)}, u32[]{:S(2)}, u32[]{:S(2)}) async-start(bf16[128,16,512]{2,0,1:T(8,128)(2,1)} %copy.43), calls=%async_computation.1 | async-start | bytes 4194304 | tf_op jit(solution)/shard_map/all_to_all | solution.py:173
  25.6 2.6 mul.179
  28.2 5.5 %mul.180 = f32[512,4,512]{2,0,1:T(8,128)} reshape(f32[16,32,4,4,128]{4,3,1,0,2:T(4,128)} %mul.179) | data formatting | bytes 8388608 | tf_op jit(solution)/shard_map/mul | solution.py:38
  35.2 15.2 %all-to-all-done.1 = bf16[128,16,512]{2,0,1:T(8,128)(2,1)S(1)} async-done(((bf16[128,16,512]{2,0,1:T(8,128)(2,1)}), bf16[128,16,512]{2,0,1:T(8,128)(2,1)S(1)}, u32[]{:S(2)}, u32[]{:S(2)}) %all-to-all-start.1) | async-done | bytes 2097184 | tf_op jit(solution)/shard_map/all_to_all | solution.py:173
  55.7 4.4 %collective-permute-done = f32[3,4,512]{2,0,1:T(4,128)S(1)} collective-permute-done((f32[3,4,512]{2,0,1:T(4,128)S(1)}, f32[3,4,512]{2,0,1:T(4,128)S(1)}, u32[]{:S(2)}, u32[]{:S(2)}) %collective-permute-start) | collective-permute-done | bytes 24608 | tf_op jit(solution)/shard_map/ppermute | solution.py:17
  60.1 2.5 divide_multiply_fusion
  65.3 4.7 %select_negate_fusion = f32[4,8,128,128]{3,2,1,0:T(8,128)S(1)} fusion(f32[4,128,8,128]{3,1,0,2:T(8,128)S(1)} %bitcast.175, f32[4,8,128]{2,1,0:T(8,128)S(1)} %bitcast.187, f32[4,8,128]{2,1,0:T(8,128)S(1)} %reduce_window_sum.11, pred[128,128]{1,0:T(8,128)(4,1)S(1)} %get-tuple-element.232, pred[128,128]{1,0:T(8,128)(4,1)S(1)} %get-tuple-element.233), kind=kOutput, calls=%fused_computation.62 | convolution fusion | flops 808976384 | bytes 4259840 | tf_op jit(solution)/shard_map/...cd,...ed->...ce/dot_general | solution.py:99
  72.2 2.6 add_add_fusion
  77.0 2.6 fusion.78
  90.4 3.6 %fusion.82 = f32[4,8,128,128]{3,2,1,0:T(8,128)} fusion(f32[4,8,128,128]{3,2,1,0:T(8,128)S(1)} %fusion.81), kind=kOutput, calls=%fused_computation.125 | convolution fusion | flops 805306368 | bytes 4194304 | tf_op jit(solution)/shard_map/...ij,...jk->...ik/dot_general | solution.py:83
  94.0 3.7 %convolution_add_fusion.3 = f32[4,8,128,128]{3,2,1,0:T(8,128)} fusion(f32[4,8,128,128]{3,2,1,0:T(8,128)S(1)} %fusion.81, f32[4,8,128,128]{3,2,1,0:T(8,128)S(1)} %convolution_add_fusion.4, f32[4,8,128,128]{3,2,1,0:T(8,128)S(1)} %fusion.80), kind=kOutput, calls=%fused_computation.67 | convolution fusion | flops 806354944 | bytes 8388608 | tf_op jit(solution)/shard_map/...ij,...jk->...ik/dot_general | solution.py:84
  97.7 2.7 copy.50
  100.4 3.0 reshape_reshape.11
  110.9 4.3 %fusion.25 = f32[4,8,128,256]{3,2,1,0:T(8,128)S(1)} fusion(f32[4,8,128,128]{3,2,1,0:T(8,128)S(1)} %get-tuple-element.215, f32[4,8,128,128]{3,2,1,0:T(8,128)S(1)} %bitcast_multiply_fusion.2, f32[4,8,128,128]{3,2,1,0:T(8,128)S(1)} %copy-done.7, f32[4,8,128,128]{3,2,1,0:T(8,128)S(1)} %fusion.83), kind=kOutput, calls=%fused_computation.37 | convolution fusion | flops 1612185600 | bytes 12582912 | tf_op jit(solution)/shard_map/...ce,...ed->...cd/dot_general | solution.py:106
  117.9 2.9 copy.52
  120.8 18.2 %while.37 = (s32[]{:T(128)}, f32[8,128,256]{2,1,0:T(8,128)S(1)}, f32[4,8]{1,0:T(4,128)S(1)}, f32[4,8,128,128]{2,3,1,0:T(8,128)}, f32[4,8,128,128]{3,2,1,0:T(8,128)S(1)}, /*index=5*/f32[4,8,128,128]{3,2,1,0:T(8,128)}) while((s32[]{:T(128)}, f32[8,128,256]{2,1,0:T(8,128)S(1)}, f32[4,8]{1,0:T(4,128)S(1)}, ...), condition=%wide.region_4.5_spmd.clone, body=%wide.region_3.4_spmd.sunk.clone | while | flops 806092800 | bytes 7865517 | solution.py:192
  122.9 2.4 convolution_add_fusion.11
  127.5 2.4 convolution_add_fusion.11
  132.0 2.4 convolution_add_fusion.11
  136.6 2.4 convolution_add_fusion.11
  143.7 5.8 %fusion.31 = f32[4,8,128,128]{3,2,1,0:T(8,128)} fusion(f32[4,8,128,128]{3,2,0,1:T(8,128)S(1)} %bitcast.178, f32[4,128,8,128]{3,1,0,2:T(8,128)S(1)} %bitcast.177), kind=kOutput, calls=%fused_computation.48 | convolution fusion | flops 805306368 | bytes 6291456 | tf_op jit(solution)/shard_map/...cd,...ed->...ce/dot_general | solution.py:110
  149.5 61.5 %all-gather.5.cloned.1.call-done = f32[64,128,128]{2,1,0:T(8,128)} async-done(((f32[8,128,128]{2,1,0:T(8,128)}), f32[64,128,128]{2,1,0:T(8,128)}) %all-gather.5.cloned.1.call-update) | async-done | bytes 4194320 | tf_op jit(solution)/shard_map/all_gather | solution.py:22
  211.0 73.8 %all-gather.7.cloned.1.call-done = f32[64,128,128]{2,1,0:T(8,128)} async-done(((f32[8,128,128]{2,1,0:T(8,128)}), f32[64,128,128]{2,1,0:T(8,128)}) %all-gather.7.cloned.1.call-update) | async-done | bytes 4194320 | tf_op jit(solution)/shard_map/all_gather | solution.py:22
  284.8 13.5 %while.38 = (s32[]{:T(128)}, f32[8,128,128]{2,1,0:T(8,128)S(1)}, s32[]{:T(128)}, f32[8,8,128,128]{3,2,1,0:T(8,128)}, f32[8,8,128,128]{3,2,1,0:T(8,128)}) while((s32[]{:T(128)}, f32[8,128,128]{2,1,0:T(8,128)S(1)}, s32[]{:T(128)}, f32[8,8,128,128]{3,2,1,0:T(8,128)}, f32[8,8,128,128]{3,2,1,0:T(8,128)}) %tuple.95), condition=%wide.region_6.7_spmd.clone, body=%wide.region_5.6_spmd.sunk.clone | while | flops 201457664 | bytes 3146847 | solution.py:30
  298.3 18.0 %while.39 = (s32[]{:T(128)}, f32[8,128,128]{2,1,0:T(8,128)S(1)}, f32[4,8,128,128]{3,2,1,0:T(8,128)}, f32[4,8]{1,0:T(4,128)S(1)}, f32[4,8,128,128]{2,3,1,0:T(8,12...) while((s32[]{:T(128)}, f32[8,128,128]{2,1,0:T(8,128)S(1)}, ...), condition=%wide.region_8.9_spmd.clone, body=%wide.region_7.8_spmd.sunk.clone | while | flops 403046400 | bytes 5245105 | solution.py:197
  316.4 4.5 %fusion.69 = f32[4,8,128,128]{3,2,1,0:T(8,128)S(1)} fusion(f32[4,8,128,128]{3,2,1,0:T(8,128)} %get-tuple-element.120, f32[4,8,128,256]{3,2,1,0:T(8,128)} %copy-done), kind=kOutput, calls=%fused_computation.112 | convolution fusion | flops 805306368 | bytes 6291456 | tf_op jit(solution)/shard_map/...ck,...kv->...cv/dot_general | solution.py:124
  321.0 2.6 fusion.38
  323.6 2.8 multiply_reduce_fusion
  327.8 17.0 %all_to_all.46 = bf16[512,8,128]{2,1,0:T(8,128)(2,1)S(1)} all-to-all(bf16[512,8,128]{2,1,0:T(8,128)(2,1)S(1)} %bitcast.181), channel_id=1, replica_groups=mesh['outer'=8,'inner'=4] {'inner'}, dimensions={0} | all-to-all | bytes 2097152 | tf_op jit(solution)/shard_map/all_to_all | solution.py:206
  (131 shorter events, 82.8 us)
Async XLA Ops:
  13.8 7.4 %all-to-all-start = ((bf16[128,16,4]{0,2,1:T(4,128)(2,1)}), bf16[128,16,4]{0,2,1:T(4,128)(2,1)S(1)}, u32[]{:S(2)}, u32[]{:S(2)}) async-start(bf16[128,16,4]{0,2,1:T(4,128)(2,1)} %param.15), calls=%async_computation | async-start | bytes 32768 | tf_op jit(solution)/shard_map/all_to_all | solution.py:175
  21.2 29.3 %all-to-all-start.1 = ((bf16[128,16,512]{2,0,1:T(8,128)(2,1)}), bf16[128,16,512]{2,0,1:T(8,128)(2,1)S(1)}, u32[]{:S(2)}, u32[]{:S(2)}) async-start(bf16[128,16,512]{2,0,1:T(8,128)(2,1)} %copy.43), calls=%async_computation.1 | async-start | bytes 4194304 | tf_op jit(solution)/shard_map/all_to_all | solution.py:173
  24.8 0.7 copy-start.15
  24.8 0.8 copy-start.12
  24.8 186.2 %all-gather.5.cloned.1.call-start = ((), (), s32[]{:S(2)}) async-start(), calls=%async_computation.4 | async-start | bytes 4718592 | tf_op jit(solution)/shard_map/all_gather | solution.py:22
  28.2 5.6 %copy-start.13 = (f32[8]{0:T(128)S(1)}, f32[8]{0:T(128)}, u32[]{:S(2)}) copy-start(f32[8]{0:T(128)} %param.18) | copy-start | bytes 100
  51.0 2.2 copy-start.8
  54.3 5.8 %collective-permute-start = (f32[3,4,512]{2,0,1:T(4,128)S(1)}, f32[3,4,512]{2,0,1:T(4,128)S(1)}, u32[]{:S(2)}, u32[]{:S(2)}) collective-permute-start(f32[3,4,512]{2,0,1:T(4,128)S(1)} %slice.73), channel_id=1, source_target_pairs={{0,4},{4,8},{8,12},{12,16},{16,20},{20,24},{24,28},{1,5},{5,9},{9,... | collective-permute-start | bytes 73736 | tf_op jit(solution)/shard_map/ppermute | solution.py:17
  62.6 14.4 %copy-start.2 = (f32[512,4,512]{2,0,1:T(8,128)}, f32[512,4,512]{2,0,1:T(8,128)S(1)}, u32[]{:S(2)}) copy-start(f32[512,4,512]{2,0,1:T(8,128)S(1)} %divide_multiply_fusion) | copy-start | bytes 12582916
  65.3 43.3 %copy-start.3 = (f32[512,4,2,128]{3,0,2,1:T(8,128)}, f32[512,4,2,128]{3,0,2,1:T(8,128)S(1)}, u32[]{:S(2)}) copy-start(f32[512,4,2,128]{3,0,2,1:T(8,128)S(1)} %broadcast_in_dim.49) | copy-start | bytes 6291460
  94.0 3.7 %slice-start = ((f32[512,4,512]{2,0,1:T(8,128)}), f32[512,4,256]{2,0,1:T(8,128)S(1)}, s32[]{:S(2)}) async-start(f32[512,4,512]{2,0,1:T(8,128)} %copy-done.2), calls=%async_computation.6 | async-start | bytes 4194304 | tf_op jit(solution)/shard_map/slice | solution.py:59
  103.4 2.3 copy-start.7
  103.4 2.9 copy-start.9
  115.3 2.6 copy-start
  140.1 144.7 %all-gather.7.cloned.1.call-start = ((), (), s32[]{:S(2)}) async-start(), calls=%async_computation.5 | async-start | bytes 4718592 | tf_op jit(solution)/shard_map/all_gather | solution.py:22
  140.8 2.9 copy-start.4
  142.4 1.3 copy-start.5
  316.4 4.5 %copy-start.1 = (f32[4,8,128,256]{3,2,1,0:T(8,128)S(1)}, f32[4,8,128,256]{3,2,1,0:T(8,128)}, u32[]{:S(2)}) copy-start(f32[4,8,128,256]{3,2,1,0:T(8,128)} %copy-done) | copy-start | bytes 12582916
  316.4 4.5 %copy-start.10 = (f32[4,8,128,128]{3,2,1,0:T(8,128)S(1)}, f32[4,8,128,128]{3,2,1,0:T(8,128)}, u32[]{:S(2)}) copy-start(f32[4,8,128,128]{3,2,1,0:T(8,128)} %fusion.31) | copy-start | bytes 6291460
  320.9 2.6 copy-start.6
  320.9 2.6 copy-start.11
  323.6 2.8 copy-start.14
Sparse Core Ops, SparseCore 0:
  140.2 70.7 all-gather.4
  213.1 71.6 all-gather.6
where the time goes:
time: 360 us; the launch traced here: 353 us
  waiting for transfers between devices  156 us (43%)
  matrix products  99.6 us (28%)
  local copies, waits for them, and re-layouts  37.8 us (10%)
  blocking collectives  23.4 us (6%)
  between operations  14.4 us (4%)
  other arithmetic  13.4 us (4%)
  starting transfers between devices  8.24 us (2%)
    all_gather x2, waiting for transfers between devices, carried_in(): gathered = jax.tree.map(lambda a: lax.all_gather(a, axis), part)  135 us
    dot_general x8, matrix products, advance(): jnp.einsum('...ck,...cv->...kv', carried_keys, incoming_value_rows, preci...  17 us
    all_to_all x1, blocking collectives, local(): lax.all_to_all(by_token, 'inner', split_axis=0, concat_axis=1, tiled=True)  17 us
    dot_general x6, matrix products, lower_inverse(): jnp.einsum('...ij,...jk->...ik', inverse, power, precision=HIGH_PRECISION)  15.3 us
    all_to_all x1, waiting for transfers between devices, local(): lax.all_to_all(qkv_blocks, 'inner', split_axis=1, concat_axis=0, tiled=True)  15.2 us
    dot_general x6, matrix products, lower_inverse(): jnp.einsum('...ij,...jk->...ik', power, power, precision=HIGH_PRECISION)  14.5 us
    dot_general x7, matrix products, compose(): jnp.einsum('hij,hjk->hik', trans_late, state_early, precision=HIGH_PRECIS...  13 us
    unnamed x34, local copies, waits for them, and re-layouts  9.55 us
  transfers between devices with their start and end apart: 5, of which 4 were waited for; matrix products, arithmetic and copies ran while one was open for 6% of the time, Pallas kernels for 0%

commit v1 on v0

--- a/solution.py
+++ b/solution.py
@@ -9,6 +9,14 @@
 CONV = 4
 HIGH_PRECISION = lax.Precision.HIGHEST
 EPS_NORM = 1e-06
+
+
+def _treat_thing(mat):
+    arr_now = lax.axis_size("inner")
+    clean = jnp.split(mat, arr_now, axis=0)
+    w_next = jnp.stack(clean, axis=0)
+    v_next = lax.all_to_all(w_next, "inner", 0, 0)
+    return jnp.concatenate(v_next, axis=1)
 
 
 def from_behind(value, axis, steps):
@@ -203,7 +211,7 @@
     )
     normed = scaled.astype(jnp.bfloat16)
     by_token = jnp.swapaxes(normed, 1, 2).reshape(token_count, head_count, HD)
-    return lax.all_to_all(by_token, "inner", split_axis=0, concat_axis=1, tiled=True)
+    return _treat_thing(by_token)
 
 
 def solution(mesh):

time: 360 us -> 363 us (level)
  no operation moved by 1% of the time
where the time goes in v1:
time: 363 us; the launch traced here: 356 us
  waiting for transfers between devices  156 us (43%)
  matrix products  103 us (28%)
  local copies, waits for them, and re-layouts  37.6 us (10%)
  blocking collectives  23.4 us (6%)
  between operations  14.4 us (4%)
  other arithmetic  13.1 us (4%)
  starting transfers between devices  8.24 us (2%)
    all_gather x2, waiting for transfers between devices, carried_in(): gathered = jax.tree.map(lambda a: lax.all_gather(a, axis), part)  135 us
    dot_general x8, matrix products, advance(): jnp.einsum('...ck,...cv->...kv', carried_keys, incoming_value_rows, preci...  17 us
    all_to_all x1, blocking collectives, _treat_thing(): v_next = lax.all_to_all(w_next, 'inner', 0, 0)  17 us
    dot_general x6, matrix products, lower_inverse(): jnp.einsum('...ij,...jk->...ik', inverse, power, precision=HIGH_PRECISION)  15.3 us
    all_to_all x1, waiting for transfers between devices, local(): lax.all_to_all(qkv_blocks, 'inner', split_axis=1, concat_axis=0, tiled=True)  15.2 us
    dot_general x6, matrix products, lower_inverse(): jnp.einsum('...ij,...jk->...ik', power, power, precision=HIGH_PRECISION)  14.5 us
    dot_general x7, matrix products, compose(): jnp.einsum('hij,hjk->hik', trans_late, state_early, precision=HIGH_PRECIS...  13 us
    unnamed x34, local copies, waits for them, and re-layouts  9.55 us
  transfers between devices with their start and end apart: 5, of which 4 were waited for; matrix products, arithmetic and copies ran while one was open for 6% of the time, Pallas kernels for 0%

profile of v1, /device:TPU:28, one launch (start us, length us, event | category | flops | bytes accessed | tf_op | source)
XLA Modules:
  0.0 355.7 jit_solution(11261421237030955748)
XLA Ops:
  7.3 6.4 %all_to_all.32 = bf16[4,16,4]{2,0,1:T(4,128)(2,1)S(1)} all-to-all(bf16[4,16,4]{2,0,1:T(4,128)(2,1)S(1)} %copy.51), channel_id=1, replica_groups=mesh['outer'=8,'inner'=4] {'inner'}, dimensions={1} | all-to-all | bytes 1024 | tf_op jit(solution)/shard_map/all_to_all | solution.py:182
  13.8 3.3 all-to-all-start
  17.0 4.1 %copy.49 = bf16[128,16,512]{2,0,1:T(8,128)(2,1)} copy(bf16[128,16,512]{2,1,0:T(8,128)(2,1)} %param.13) | data formatting | bytes 4194304 | tf_op args[0]
  21.2 3.6 %all-to-all-start.1 = ((bf16[128,16,512]{2,0,1:T(8,128)(2,1)}), bf16[128,16,512]{2,0,1:T(8,128)(2,1)S(1)}, u32[]{:S(2)}, u32[]{:S(2)}) async-start(bf16[128,16,512]{2,0,1:T(8,128)(2,1)} %copy.49), calls=%async_computation.1 | async-start | bytes 4194304 | tf_op jit(solution)/shard_map/all_to_all | solution.py:181
  25.6 2.6 mul.179
  28.2 5.5 %mul.180 = f32[512,4,512]{2,0,1:T(8,128)} reshape(f32[16,32,4,4,128]{4,3,1,0,2:T(4,128)} %mul.179) | data formatting | bytes 8388608 | tf_op jit(solution)/shard_map/mul | solution.py:46
  35.2 15.2 %all-to-all-done.1 = bf16[128,16,512]{2,0,1:T(8,128)(2,1)S(1)} async-done(((bf16[128,16,512]{2,0,1:T(8,128)(2,1)}), bf16[128,16,512]{2,0,1:T(8,128)(2,1)S(1)}, u32[]{:S(2)}, u32[]{:S(2)}) %all-to-all-start.1) | async-done | bytes 2097184 | tf_op jit(solution)/shard_map/all_to_all | solution.py:181
  55.7 4.4 %collective-permute-done = f32[3,4,512]{2,0,1:T(4,128)S(1)} collective-permute-done((f32[3,4,512]{2,0,1:T(4,128)S(1)}, f32[3,4,512]{2,0,1:T(4,128)S(1)}, u32[]{:S(2)}, u32[]{:S(2)}) %collective-permute-start) | collective-permute-done | bytes 24608 | tf_op jit(solution)/shard_map/ppermute | solution.py:25
  60.1 2.5 divide_multiply_fusion
  65.3 4.7 %select_negate_fusion = f32[4,8,128,128]{3,2,1,0:T(8,128)S(1)} fusion(f32[4,128,8,128]{3,1,0,2:T(8,128)S(1)} %bitcast.171, f32[4,8,128]{2,1,0:T(8,128)S(1)} %bitcast.182, f32[4,8,128]{2,1,0:T(8,128)S(1)} %reduce_window_sum.11, pred[128,128]{1,0:T(8,128)(4,1)S(1)} %get-tuple-element.232, pred[128,128]{1,0:T(8,128)(4,1)S(1)} %get-tuple-element.233), kind=kOutput, calls=%fused_computation.62 | convolution fusion | flops 808976384 | bytes 4259840 | tf_op jit(solution)/shard_map/...cd,...ed->...ce/dot_general | solution.py:107
  72.2 2.6 add_add_fusion
  77.0 2.6 fusion.78
  90.4 3.6 %fusion.82 = f32[4,8,128,128]{3,2,1,0:T(8,128)} fusion(f32[4,8,128,128]{3,2,1,0:T(8,128)S(1)} %fusion.81), kind=kOutput, calls=%fused_computation.124 | convolution fusion | flops 805306368 | bytes 4194304 | tf_op jit(solution)/shard_map/...ij,...jk->...ik/dot_general | solution.py:91
  94.0 3.7 %convolution_add_fusion.3 = f32[4,8,128,128]{3,2,1,0:T(8,128)} fusion(f32[4,8,128,128]{3,2,1,0:T(8,128)S(1)} %fusion.81, f32[4,8,128,128]{3,2,1,0:T(8,128)S(1)} %convolution_add_fusion.4, f32[4,8,128,128]{3,2,1,0:T(8,128)S(1)} %fusion.80), kind=kOutput, calls=%fused_computation.67 | convolution fusion | flops 806354944 | bytes 8388608 | tf_op jit(solution)/shard_map/...ij,...jk->...ik/dot_general | solution.py:92
  97.7 2.7 copy.56
  100.4 3.0 reshape_reshape.11
  110.9 4.3 %fusion.25 = f32[4,8,128,256]{3,2,1,0:T(8,128)S(1)} fusion(f32[4,8,128,128]{3,2,1,0:T(8,128)S(1)} %get-tuple-element.215, f32[4,8,128,128]{3,2,1,0:T(8,128)S(1)} %bitcast_multiply_fusion.2, f32[4,8,128,128]{3,2,1,0:T(8,128)S(1)} %copy-done.7, f32[4,8,128,128]{3,2,1,0:T(8,128)S(1)} %fusion.83), kind=kOutput, calls=%fused_computation.37 | convolution fusion | flops 1612185600 | bytes 12582912 | tf_op jit(solution)/shard_map/...ce,...ed->...cd/dot_general | solution.py:114
  117.9 2.9 copy.58
  120.8 18.2 %while.37 = (s32[]{:T(128)}, f32[8,128,256]{2,1,0:T(8,128)S(1)}, f32[4,8]{1,0:T(4,128)S(1)}, f32[4,8,128,128]{2,3,1,0:T(8,128)}, f32[4,8,128,128]{3,2,1,0:T(8,128)S(1)}, /*index=5*/f32[4,8,128,128]{3,2,1,0:T(8,128)}) while((s32[]{:T(128)}, f32[8,128,256]{2,1,0:T(8,128)S(1)}, f32[4,8]{1,0:T(4,128)S(1)}, ...), condition=%wide.region_4.5_spmd.clone, body=%wide.region_3.4_spmd.sunk.clone | while | flops 806092800 | bytes 7865517 | solution.py:200
  122.9 2.4 convolution_add_fusion.11
  127.5 2.4 convolution_add_fusion.11
  132.0 2.4 convolution_add_fusion.11
  136.6 2.4 convolution_add_fusion.11
  143.7 5.8 %fusion.31 = f32[4,8,128,128]{3,2,1,0:T(8,128)} fusion(f32[4,8,128,128]{3,2,0,1:T(8,128)S(1)} %bitcast.174, f32[4,128,8,128]{3,1,0,2:T(8,128)S(1)} %bitcast.173), kind=kOutput, calls=%fused_computation.48 | convolution fusion | flops 805306368 | bytes 6291456 | tf_op jit(solution)/shard_map/...cd,...ed->...ce/dot_general | solution.py:118
  149.5 61.5 %all-gather.5.cloned.1.call-done = f32[64,128,128]{2,1,0:T(8,128)} async-done(((f32[8,128,128]{2,1,0:T(8,128)}), f32[64,128,128]{2,1,0:T(8,128)}) %all-gather.5.cloned.1.call-update) | async-done | bytes 4194320 | tf_op jit(solution)/shard_map/all_gather | solution.py:30
  211.0 73.8 %all-gather.7.cloned.1.call-done = f32[64,128,128]{2,1,0:T(8,128)} async-done(((f32[8,128,128]{2,1,0:T(8,128)}), f32[64,128,128]{2,1,0:T(8,128)}) %all-gather.7.cloned.1.call-update) | async-done | bytes 4194320 | tf_op jit(solution)/shard_map/all_gather | solution.py:30
  284.8 13.5 %while.38 = (s32[]{:T(128)}, f32[8,128,128]{2,1,0:T(8,128)S(1)}, s32[]{:T(128)}, f32[8,8,128,128]{3,2,1,0:T(8,128)}, f32[8,8,128,128]{3,2,1,0:T(8,128)}) while((s32[]{:T(128)}, f32[8,128,128]{2,1,0:T(8,128)S(1)}, s32[]{:T(128)}, f32[8,8,128,128]{3,2,1,0:T(8,128)}, f32[8,8,128,128]{3,2,1,0:T(8,128)}) %tuple.95), condition=%wide.region_6.7_spmd.clone, body=%wide.region_5.6_spmd.sunk.clone | while | flops 201457664 | bytes 3146847 | solution.py:38
  298.3 18.0 %while.39 = (s32[]{:T(128)}, f32[8,128,128]{2,1,0:T(8,128)S(1)}, f32[4,8,128,128]{3,2,1,0:T(8,128)}, f32[4,8]{1,0:T(4,128)S(1)}, f32[4,8,128,128]{2,3,1,0:T(8,12...) while((s32[]{:T(128)}, f32[8,128,128]{2,1,0:T(8,128)S(1)}, ...), condition=%wide.region_8.9_spmd.clone, body=%wide.region_7.8_spmd.sunk.clone | while | flops 403046400 | bytes 5245105 | solution.py:205
  316.4 4.5 %fusion.69 = f32[4,8,128,128]{3,2,1,0:T(8,128)S(1)} fusion(f32[4,8,128,128]{3,2,1,0:T(8,128)} %get-tuple-element.120, f32[4,8,128,256]{3,2,1,0:T(8,128)} %copy-done), kind=kOutput, calls=%fused_computation.111 | convolution fusion | flops 805306368 | bytes 6291456 | tf_op jit(solution)/shard_map/...ck,...kv->...cv/dot_general | solution.py:132
  321.0 4.2 %fusion.38 = f32[4,8,128,128]{2,3,1,0:T(8,128)S(1)} fusion(f32[4,8,128,128]{3,2,1,0:T(8,128)S(1)} %fusion.69, f32[4,8,128,128]{3,2,1,0:T(8,128)S(1)} %copy-done.10, f32[4,8,128]{2,1,0:T(8,128)S(1)} %reduce_window_sum.11, pred[128,128]{1,0:T(8,128)(4,1)S(1)} %get-tuple-element.232, f32[4,8,128,256]{3,2,1,0:T(8,128)S(1)} %copy-done.1), kind=kOutput, calls=%fused_computation.58 | convolution fusion | flops 807927808 | bytes 8437760 | tf_op jit(solution)/shard_map/...ce,...ev->...cv/dot_general | solution.py:136
  325.1 4.2 %multiply_reduce_fusion = (f32[4,8,128]{2,1,0:T(8,128)S(1)}, f32[4,8,128,128]{2,3,1,0:T(8,128)S(1)}) fusion(f32[4,8,128,128]{2,3,1,0:T(8,128)S(1)} %fusion.38, f32[4,8,128,128]{3,2,1,0:T(8,128)S(1)} %copy-done.11, f32[4,8,128,128]{3,2,0,1:T(8,128)S(1)} %bitcast.175, f32[4,8,128]{2,0,1:T(4,128)S(1)} %copy.48), kind=kOutput, calls=%fused_computation.57 | convolution fusion | flops 807399424 | bytes 8421376 | tf_op jit(solution)/shard_map/...ck,...kv->...cv/dot_general | solution.py:135
  329.7 17.0 %all_to_all.33 = bf16[4,128,8,128]{1,3,2,0:T(8,128)(2,1)S(1)} all-to-all(bf16[4,128,8,128]{1,3,2,0:T(8,128)(2,1)S(1)} %fusion.30), channel_id=1, replica_groups=mesh['outer'=8,'inner'=4] {'inner'}, dimensions={0} | all-to-all | bytes 2097152 | tf_op jit(solution)/shard_map/all_to_all | solution.py:18
  (130 shorter events, 82.3 us)
Async XLA Ops:
  13.8 7.4 %all-to-all-start = ((bf16[128,16,4]{0,2,1:T(4,128)(2,1)}), bf16[128,16,4]{0,2,1:T(4,128)(2,1)S(1)}, u32[]{:S(2)}, u32[]{:S(2)}) async-start(bf16[128,16,4]{0,2,1:T(4,128)(2,1)} %param.15), calls=%async_computation | async-start | bytes 32768 | tf_op jit(solution)/shard_map/all_to_all | solution.py:183
  21.2 29.3 %all-to-all-start.1 = ((bf16[128,16,512]{2,0,1:T(8,128)(2,1)}), bf16[128,16,512]{2,0,1:T(8,128)(2,1)S(1)}, u32[]{:S(2)}, u32[]{:S(2)}) async-start(bf16[128,16,512]{2,0,1:T(8,128)(2,1)} %copy.49), calls=%async_computation.1 | async-start | bytes 4194304 | tf_op jit(solution)/shard_map/all_to_all | solution.py:181
  24.8 0.7 copy-start.15
  24.8 0.8 copy-start.12
  24.8 186.2 %all-gather.5.cloned.1.call-start = ((), (), s32[]{:S(2)}) async-start(), calls=%async_computation.4 | async-start | bytes 4718592 | tf_op jit(solution)/shard_map/all_gather | solution.py:30
  28.2 5.6 %copy-start.13 = (f32[8]{0:T(128)S(1)}, f32[8]{0:T(128)}, u32[]{:S(2)}) copy-start(f32[8]{0:T(128)} %param.18) | copy-start | bytes 100
  51.0 2.2 copy-start.8
  54.3 5.8 %collective-permute-start = (f32[3,4,512]{2,0,1:T(4,128)S(1)}, f32[3,4,512]{2,0,1:T(4,128)S(1)}, u32[]{:S(2)}, u32[]{:S(2)}) collective-permute-start(f32[3,4,512]{2,0,1:T(4,128)S(1)} %slice.78), channel_id=1, source_target_pairs={{0,4},{4,8},{8,12},{12,16},{16,20},{20,24},{24,28},{1,5},{5,9},{9,... | collective-permute-start | bytes 73736 | tf_op jit(solution)/shard_map/ppermute | solution.py:25
  62.6 14.4 %copy-start.2 = (f32[512,4,512]{2,0,1:T(8,128)}, f32[512,4,512]{2,0,1:T(8,128)S(1)}, u32[]{:S(2)}) copy-start(f32[512,4,512]{2,0,1:T(8,128)S(1)} %divide_multiply_fusion) | copy-start | bytes 12582916
  65.3 43.3 %copy-start.3 = (f32[512,4,2,128]{3,0,2,1:T(8,128)}, f32[512,4,2,128]{3,0,2,1:T(8,128)S(1)}, u32[]{:S(2)}) copy-start(f32[512,4,2,128]{3,0,2,1:T(8,128)S(1)} %broadcast_in_dim.49) | copy-start | bytes 6291460
  94.0 3.7 %slice-start = ((f32[512,4,512]{2,0,1:T(8,128)}), f32[512,4,256]{2,0,1:T(8,128)S(1)}, s32[]{:S(2)}) async-start(f32[512,4,512]{2,0,1:T(8,128)} %copy-done.2), calls=%async_computation.6 | async-start | bytes 4194304 | tf_op jit(solution)/shard_map/slice | solution.py:67
  103.4 2.3 copy-start.7
  103.4 2.9 copy-start.9
  115.3 2.6 copy-start
  140.1 144.7 %all-gather.7.cloned.1.call-start = ((), (), s32[]{:S(2)}) async-start(), calls=%async_computation.5 | async-start | bytes 4718592 | tf_op jit(solution)/shard_map/all_gather | solution.py:30
  140.8 2.9 copy-start.4
  142.4 1.3 copy-start.5
  316.4 4.5 %copy-start.1 = (f32[4,8,128,256]{3,2,1,0:T(8,128)S(1)}, f32[4,8,128,256]{3,2,1,0:T(8,128)}, u32[]{:S(2)}) copy-start(f32[4,8,128,256]{3,2,1,0:T(8,128)} %copy-done) | copy-start | bytes 12582916
  316.4 4.5 %copy-start.10 = (f32[4,8,128,128]{3,2,1,0:T(8,128)S(1)}, f32[4,8,128,128]{3,2,1,0:T(8,128)}, u32[]{:S(2)}) copy-start(f32[4,8,128,128]{3,2,1,0:T(8,128)} %fusion.31) | copy-start | bytes 6291460
  320.9 4.2 %copy-start.6 = (f32[512,4,2,128]{3,0,2,1:T(8,128)S(1)}, f32[512,4,2,128]{3,0,2,1:T(8,128)}, u32[]{:S(2)}) copy-start(f32[512,4,2,128]{3,0,2,1:T(8,128)} %copy-done.5) | copy-start | bytes 6291460
  320.9 4.2 %copy-start.11 = (f32[4,8,128,128]{3,2,1,0:T(8,128)S(1)}, f32[4,8,128,128]{3,2,1,0:T(8,128)}, u32[]{:S(2)}) copy-start(f32[4,8,128,128]{3,2,1,0:T(8,128)} %get-tuple-element.120) | copy-start | bytes 6291460
  325.1 4.2 %copy-start.14 = (f32[128]{0:T(128)S(1)}, f32[128]{0:T(128)}, u32[]{:S(2)}) copy-start(f32[128]{0:T(128)} %param.19) | copy-start | bytes 1540
Sparse Core Ops, SparseCore 0:
  140.2 70.7 all-gather.4
  213.1 71.6 all-gather.6
